TPU v7x, 256 devices: a whole 4x4x8 slice. The times are simulated.
256 devices in a mesh: rep: 16 (over x_hi, z), fsdp: 16 (over x_lo, y, core).
Axes of the slice: x: 4 (x_hi: 2, x_lo: 2; x = x_hi * 2 + x_lo), y: 4, z: 8, core: 2. Of those that a mesh axis runs over, the one named last changes fastest.
Arguments:
- outer_start: float32 [2048, 8192], P(None, 'fsdp'), may hold values from -6 to 6
- local_weights: bfloat16 [16, 2048, 8192], P('rep', None, 'fsdp'), may hold values from -9 to 9
- momentum: float32 [2048, 8192], P('rep', 'fsdp'), may hold values from -0.6 to 0.6
Outputs:
- new_weights: bfloat16 [2048, 8192], P(None, 'fsdp')
- new_master: float32 [2048, 8192], P('rep', 'fsdp')
- new_momentum: float32 [2048, 8192], P('rep', 'fsdp')
All inputs are finite; a program needn't handle non-finite values.
Results may differ from a plain program's by a relative error of at most 0.0045.
Values may be sent and summed in bfloat16 or wider, within the bound.
No kernel may reach another device: no remote copies, remote signals or barrier semaphores. Data moves between devices by JAX's collectives and lax.ppermute only.
A program may use at most 64 MiB of HBM per device.

v0:
```python
import jax
import jax.numpy as jnp
from jax import lax
from jax.sharding import PartitionSpec as P

D = 8192
clip_level = 0.03
outer_rate = 0.7
momentum_coef = 0.9
eps_value = 1e-06


def make_difference(outer_rows, local_rows):
    rounded = (outer_rows - local_rows.astype(jnp.float32)).astype(jnp.bfloat16)
    rounded = lax.optimization_barrier(rounded)
    return rounded.astype(jnp.float32)


def outer_update(own_outer, outer_grad, unit_squares, momentum_rows):
    factor = jnp.minimum(1.0, clip_level / jnp.sqrt(unit_squares / D + eps_value))
    clipped = outer_grad * factor[:, None]
    new_momentum = momentum_coef * momentum_rows + clipped
    new_master = own_outer - outer_rate * (clipped + momentum_coef * new_momentum)
    return (new_master, new_momentum)


def on_device(outer_start, local_weights, momentum):
    local_shard = local_weights[0]
    replicas = lax.axis_size("rep")
    owner = lax.axis_index("rep")
    own_rows = outer_start.shape[0] // replicas
    summed = lax.psum_scatter(
        make_difference(outer_start, local_shard).astype(jnp.bfloat16),
        "rep",
        scatter_dimension=0,
        tiled=True,
    ).astype(jnp.float32)
    own_outer = lax.dynamic_slice_in_dim(outer_start, owner * own_rows, own_rows, 0)
    outer_grad = summed / replicas
    unit_squares = lax.psum(jnp.sum(outer_grad * outer_grad, axis=1), "fsdp")
    new_master, new_momentum = outer_update(own_outer, outer_grad, unit_squares, momentum)
    new_weights = lax.all_gather(new_master.astype(jnp.bfloat16), "rep", axis=0, tiled=True)
    return (new_weights, new_master, new_momentum)


def solution(mesh):
    return jax.shard_map(
        on_device,
        mesh=mesh,
        in_specs=(P(None, "fsdp"), P("rep", None, "fsdp"), P("rep", "fsdp")),
        out_specs=(P(None, "fsdp"), P("rep", "fsdp"), P("rep", "fsdp")),
        check_vma=False,
    )
```

profile of v0, /device:TPU:8, one launch (start us, length us, event | category | flops | bytes accessed | tf_op | source)
XLA Modules:
  0.0 344.7 jit_solution(3331967806520791519)
XLA Ops:
  7.2 0.0 reduce-scatter.2.cloned.1.call-start
  7.2 4.9 %fusion = bf16[2048,512]{1,0:T(8,128)(2,1)} fusion(f32[2048,512]{1,0:T(8,128)} %param.3, bf16[1,2048,512]{2,1,0:T(8,128)(2,1)} %param.4), kind=kLoop, calls=%fused_computation.1 | loop fusion | flops 3145728 | bytes 8388608 | tf_op jit(solution)/shard_map/convert_element_type | solution.py:14
  12.1 0.0 copy-start
  12.1 0.0 reduce-scatter.2.cloned.1.call-update
  12.1 0.0 all-gather.2.cloned.1.call-start
  12.2 211.4 %reduce-scatter.2.cloned.1.call-done = bf16[128,512]{1,0:T(8,128)(2,1)} async-done(((bf16[2048,512]{1,0:T(8,128)(2,1)}), bf16[128,512]{1,0:T(8,128)(2,1)}) %reduce-scatter.2.cloned.1.call-update) | async-done | bytes 131088 | tf_op jit(solution)/shard_map/reduce_scatter | solution.py:32
  223.6 1.0 fusion.6
  224.6 23.3 %psum.7 = f32[128]{0:T(128)S(1)} all-reduce(f32[128]{0:T(128)S(1)} %fusion.6), channel_id=1, replica_groups=mesh['rep'=16,'fsdp'=16] {'fsdp'}, use_global_device_ids=true, to_apply=%region_2.0 | all-reduce | flops 128 | bytes 1024 | tf_op jit(solution)/shard_map/psum | solution.py:40
  247.9 0.0 copy-done
  247.9 2.0 fusion.7
  249.9 0.0 all-gather.2.cloned.1.call-update
  249.9 84.9 %all-gather.2.cloned.1.call-done = bf16[2048,512]{1,0:T(8,128)(2,1)} async-done(((bf16[128,512]{1,0:T(8,128)(2,1)}), bf16[2048,512]{1,0:T(8,128)(2,1)}) %all-gather.2.cloned.1.call-update) | async-done | bytes 2097168 | tf_op jit(solution)/shard_map/all_gather | solution.py:42
  334.8 3.0 copy.7
  (1 shorter events, 0.0 us)
Async XLA Ops:
  7.2 216.4 %reduce-scatter.2.cloned.1.call-start = ((), (), s32[]{:S(2)}) async-start(), calls=%async_computation.1 | async-start | bytes 2228224 | tf_op jit(solution)/shard_map/reduce_scatter | solution.py:32
  12.1 235.8 %copy-start = (f32[128,512]{1,0:T(8,128)S(1)}, f32[128,512]{1,0:T(8,128)}, u32[]{:S(2)}) copy-start(f32[128,512]{1,0:T(8,128)} %param.5) | copy-start | bytes 786436
  12.1 322.7 %all-gather.2.cloned.1.call-start = ((), (), s32[]{:S(2)}) async-start(), calls=%async_computation.2 | async-start | bytes 2228224 | tf_op jit(solution)/shard_map/all_gather | solution.py:42
Sparse Core Ops, SparseCore 0:
  12.5 211.0 reduce-scatter.1
  250.0 84.7 all-gather.1
where the time goes:
time: 345 us
  waiting for transfers between devices  296 us (86%)
  blocking collectives  23.3 us (7%)
  between operations  14 us (4%)
  other arithmetic  7.92 us (2%)
    reduce_scatter x1, waiting for transfers between devices, on_device(): lax.psum_scatter(make_difference(outer_start, local_shard).astype(jnp.bfl...  211 us
    all_gather x1, waiting for transfers between devices, on_device(): lax.all_gather(new_master.astype(jnp.bfloat16), 'rep', axis=0, tiled=True)  84.9 us
    psum x1, blocking collectives, on_device(): unit_squares = lax.psum(jnp.sum(outer_grad * outer_grad, axis=1), 'fsdp')  23.3 us
  transfers between devices with their start and end apart: 2, of which 2 were waited for; matrix products, arithmetic and copies ran while one was open for 0% of the time, Pallas kernels for 0%

commit v1 on v0

--- a/solution.py
+++ b/solution.py
@@ -39,7 +39,12 @@
     outer_grad = summed / replicas
     unit_squares = lax.psum(jnp.sum(outer_grad * outer_grad, axis=1), "fsdp")
     new_master, new_momentum = outer_update(own_outer, outer_grad, unit_squares, momentum)
-    new_weights = lax.all_gather(new_master.astype(jnp.bfloat16), "rep", axis=0, tiled=True)
+    new_weights = jnp.concatenate(
+        lax.all_to_all(
+            jnp.stack([new_master.astype(jnp.bfloat16)] * lax.axis_size("rep")), "rep", 0, 0
+        ),
+        axis=0,
+    )
     return (new_weights, new_master, new_momentum)
 
 

time: 345 us -> 318 us (0.922)
  waiting for transfers between devices: 296 us -> 211 us
  blocking collectives: 23.3 us -> 79.7 us
    all_gather x1 -> x0, waiting for transfers between devices: 84.9 us -> none  [on_device(): lax.all_gather(new_master.astype(jnp.bfloat16), 'rep', axis=0, tiled=True)]
    all_to_all x0 -> x1, blocking collectives: none -> 56.4 us  [on_device(): lax.all_to_all(jnp.stack([new_master.astype(jnp.bfloat16)] * lax.axis_siz...]
  transfers between devices with their start and end apart: 2 -> 1, of which waited for: 2 -> 1; matrix products, arithmetic and copies ran while one was open for 0% -> 0% of each run, Pallas kernels for 0% -> 0%
where the time goes in v1:
time: 318 us; the launch traced here: 315 us
  waiting for transfers between devices  211 us (66%)
  blocking collectives  79.7 us (25%)
  between operations  14 us (4%)
  other arithmetic  7.88 us (2%)
    reduce_scatter x1, waiting for transfers between devices, on_device(): lax.psum_scatter(make_difference(outer_start, local_shard).astype(jnp.bfl...  211 us
    all_to_all x1, blocking collectives, on_device(): lax.all_to_all(jnp.stack([new_master.astype(jnp.bfloat16)] * lax.axis_siz...  56.4 us
    psum x1, blocking collectives, on_device(): unit_squares = lax.psum(jnp.sum(outer_grad * outer_grad, axis=1), 'fsdp')  23.3 us
  transfers between devices with their start and end apart: 1, of which 1 were waited for; matrix products, arithmetic and copies ran while one was open for 0% of the time, Pallas kernels for 0%

profile of v1, /device:TPU:8, one launch (start us, length us, event | category | flops | bytes accessed | tf_op | source)
XLA Modules:
  0.0 314.6 jit_solution(8097090104500927170)
XLA Ops:
  7.2 0.0 reduce-scatter.2.cloned.1.call-start
  7.2 4.9 %fusion = bf16[2048,512]{1,0:T(8,128)(2,1)} fusion(f32[2048,512]{1,0:T(8,128)} %param.3, bf16[1,2048,512]{2,1,0:T(8,128)(2,1)} %param.4), kind=kLoop, calls=%fused_computation.1 | loop fusion | flops 3145728 | bytes 8388608 | tf_op jit(solution)/shard_map/convert_element_type | solution.py:14
  12.1 0.0 copy-start
  12.1 0.0 reduce-scatter.2.cloned.1.call-update
  12.1 211.4 %reduce-scatter.2.cloned.1.call-done = bf16[128,512]{1,0:T(8,128)(2,1)} async-done(((bf16[2048,512]{1,0:T(8,128)(2,1)}), bf16[128,512]{1,0:T(8,128)(2,1)}) %reduce-scatter.2.cloned.1.call-update) | async-done | bytes 131088 | tf_op jit(solution)/shard_map/reduce_scatter | solution.py:32
  223.6 1.0 fusion.6
  224.6 23.3 %psum.7 = f32[128]{0:T(128)S(1)} all-reduce(f32[128]{0:T(128)S(1)} %fusion.6), channel_id=1, replica_groups=mesh['rep'=16,'fsdp'=16] {'fsdp'}, use_global_device_ids=true, to_apply=%region_2.0 | all-reduce | flops 128 | bytes 1024 | tf_op jit(solution)/shard_map/psum | solution.py:40
  247.9 0.0 copy-done
  247.9 1.9 fusion.7
  249.8 0.2 stack.2
  250.0 56.4 %all_to_all.5 = bf16[16,128,512]{2,1,0:T(8,128)(2,1)S(1)} all-to-all(bf16[16,128,512]{2,1,0:T(8,128)(2,1)S(1)} %stack.2), channel_id=1, replica_groups=mesh['rep'=16,'fsdp'=16] {'rep'}, dimensions={0} | all-to-all | bytes 4194304 | tf_op jit(solution)/shard_map/all_to_all | solution.py:43
  306.5 1.3 copy.7
  (1 shorter events, 0.0 us)
Async XLA Ops:
  7.2 216.4 %reduce-scatter.2.cloned.1.call-start = ((), (), s32[]{:S(2)}) async-start(), calls=%async_computation.2 | async-start | bytes 2228224 | tf_op jit(solution)/shard_map/reduce_scatter | solution.py:32
  12.1 235.8 %copy-start = (f32[128,512]{1,0:T(8,128)S(1)}, f32[128,512]{1,0:T(8,128)}, u32[]{:S(2)}) copy-start(f32[128,512]{1,0:T(8,128)} %param.5) | copy-start | bytes 786436
Sparse Core Ops, SparseCore 0:
  12.5 211.0 reduce-scatter.1
